TPU v7x, 128 devices: a whole 4x4x4 slice. The times are simulated.
128 devices in a mesh: sample: 8 (over x, y_hi), landmark: 16 (over z, y_lo, core).
Axes of the slice: x: 4, y: 4 (y_hi: 2, y_lo: 2; y = y_hi * 2 + y_lo), z: 4, core: 2. Of those that a mesh axis runs over, the one named last changes fastest.
Arguments:
- summaries: bfloat16 [16384, 1024], P('sample', 'landmark'), may hold values from -12 to 12
- row_level: int32 [16384], P('sample'), may hold values from 0 to 3
- pool: bfloat16 [32768, 1024], P('landmark'), may hold values from -6 to 6
- pool_level: int32 [32768], P('landmark'), may hold values from 0 to 3
- landmark_index: int32 [16384], P('landmark'), may hold values from 0 to 2047, as said below
- level_scale: float32 [4], replicated, may hold values from 1.2 to 2.4
- targets: bfloat16 [16384, 256], P('sample'), may hold values from -6 to 6
Outputs:
- weights: float32 [16384, 256], P('landmark')
- residual: float32 [16384, 256], P('landmark')
Inputs may be any that keep to these rules, and one draw needn't show every extreme that they name: Landmark j is pool row (j // 1024) * 2048 + landmark_index[j], a row of the pool block of its own landmark group; indices may repeat.
All inputs are finite; a program needn't handle non-finite values.
Results may differ from a plain program's by a relative error of at most 0.012.
Values may be sent and summed in bfloat16 or wider, within the bound.
No kernel may reach another device: no remote copies, remote signals or barrier semaphores. Data moves between devices by JAX's collectives and lax.ppermute only.
A program may use at most 64 MiB of HBM per device.

v0:
```python
import math
import jax
import jax.numpy as jnp
from jax import lax
from jax.sharding import PartitionSpec as P

ITERS = 2
GROUPS = 1


def REDUCE(x, extra, axis, bits, gather_dtype, wire_dtype=jnp.bfloat16):
    return exchange_sum(x, extra, axis, gather_dtype, wire_dtype)


ridge = 0.5


def level_values(level_ids, level_table):
    onehot = level_ids[:, None] == jnp.arange(level_table.shape[0], dtype=jnp.int32)[None, :]
    return jnp.sum(
        jnp.where(onehot, level_table[None, :], jnp.zeros_like(level_table)[None, :]), axis=1
    )


def raw_block(summary_rows, row_factor, anchors, anchor_factor):
    scores = jnp.dot(summary_rows, anchors.T, preferred_element_type=jnp.float32)
    return jnp.exp(scores * row_factor[:, None] * anchor_factor[None, :])


def partner_bits(size, order):
    bits = [b for b in order if b < size]
    assert sorted(bits) == [1 << i for i in range(size.bit_length() - 1)]
    return bits


def butterfly_sum(x, axis, bits):
    size = lax.axis_size(axis)
    for k in bits:
        perm = [(i, i ^ k) for i in range(size)]
        x = x + lax.ppermute(x, axis, perm)
    return x


def pack_rows(extra, columns, wire_dtype):
    rows = extra.reshape(-1, columns)
    if wire_dtype == jnp.float32:
        parts = [rows]
    else:
        parts = []
        rest = rows
        for _ in range(3):
            term = lax.reduce_precision(rest, exponent_bits=8, mantissa_bits=7)
            parts.append(term)
            rest = rest - term
    return jnp.concatenate(parts, axis=0).astype(wire_dtype)


def unpack_rows(packed, count, wire_dtype):
    terms = 1 if wire_dtype == jnp.float32 else 3
    packed = packed.astype(jnp.float32).reshape(terms, count, -1)
    total = packed[0]
    for t in range(1, terms):
        total = total + packed[t]
    return total.reshape(-1)


def halving_sum(x, extra, axis, bits, gather_dtype, wire_dtype=jnp.bfloat16):
    size = lax.axis_size(axis)
    index = lax.axis_index(axis)
    columns = x.shape[1]
    for k in bits:
        perm = [(i, i ^ k) for i in range(size)]
        half = x.shape[0] // 2
        mine = index // k % 2
        keep = lax.dynamic_slice_in_dim(x, mine * half, half, axis=0)
        send = lax.dynamic_slice_in_dim(x, (1 - mine) * half, half, axis=0).astype(wire_dtype)
        if extra is not None:
            send = jnp.concatenate([send, pack_rows(extra, columns, wire_dtype)], axis=0)
        got = lax.ppermute(send, axis, perm)
        x = keep + got[:half].astype(jnp.float32)
        if extra is not None:
            extra = extra + unpack_rows(got[half:], extra.shape[0] // columns, wire_dtype)
    x = x.astype(gather_dtype)
    for k in reversed(bits):
        perm = [(i, i ^ k) for i in range(size)]
        part = x.shape[0]
        mine = index // k % 2
        got = lax.ppermute(x, axis, perm)
        whole = jnp.zeros((2 * part,) + x.shape[1:], x.dtype)
        whole = lax.dynamic_update_slice_in_dim(whole, x, mine * part, axis=0)
        x = lax.dynamic_update_slice_in_dim(whole, got, (1 - mine) * part, axis=0)
    return (x, extra)


def exchange_scatter(x, extra, axis, wire_dtype):
    size = lax.axis_size(axis)
    rows, columns = x.shape
    chunks = x.reshape(size, rows // size, columns).astype(wire_dtype)
    if extra is not None:
        packed = pack_rows(extra, columns, wire_dtype)
        chunks = jnp.concatenate(
            [chunks, jnp.broadcast_to(packed[None], (size,) + packed.shape)], axis=1
        )
    got = lax.all_to_all(chunks, axis, 0, 0, tiled=False)
    total = jnp.sum(got.astype(jnp.float32), axis=0)
    part = total[: rows // size]
    if extra is not None:
        extra = unpack_rows(total[rows // size :], extra.shape[0] // columns, wire_dtype)
    return (part, extra)


def exchange_gather(part, axis):
    size = lax.axis_size(axis)
    whole = lax.all_to_all(
        jnp.broadcast_to(part[None], (size,) + part.shape), axis, 0, 0, tiled=False
    )
    return whole.reshape((size * part.shape[0],) + part.shape[1:])


def exchange_sum(x, extra, axis, gather_dtype, wire_dtype=jnp.bfloat16):
    part, extra = exchange_scatter(x, extra, axis, wire_dtype)
    return (exchange_gather(part.astype(gather_dtype), axis), extra)


def native_scatter(x, extra, axis):
    size = lax.axis_size(axis)
    rows, columns = x.shape
    chunks = x.reshape(size, rows // size, columns)
    packed = extra.reshape(-1, columns)
    chunks = jnp.concatenate(
        [chunks, jnp.broadcast_to(packed[None], (size,) + packed.shape)], axis=1
    )
    total = lax.psum_scatter(chunks, axis, scatter_dimension=0, tiled=False)
    return (total[: rows // size], total[rows // size :].reshape(-1))


def native_gather(part, axis):
    return lax.all_gather(part, axis, axis=0, tiled=True)


def conjugate_gradients(kernel, targets, n_rows, sample_bits, landmark_bits):
    rhs_part = jnp.dot(kernel.T, targets, preferred_element_type=jnp.float32)
    rhs_total, _ = exchange_sum(rhs_part, None, "sample", jnp.float32, jnp.float32)
    rhs = rhs_total / math.sqrt(n_rows)
    column_count = rhs.shape[1]
    weights = jnp.zeros_like(rhs)
    residual = rhs
    direction = rhs
    for iteration in range(ITERS):
        if iteration == 0:
            row_part = jnp.dot(
                kernel, direction.astype(jnp.bfloat16), preferred_element_type=jnp.float32
            )
            sums = jnp.concatenate(
                [jnp.sum(direction * direction, axis=0), jnp.sum(residual * residual, axis=0)]
            )
            row_chunk, landmark_sums = native_scatter(row_part, sums, "landmark")
            direction_square = landmark_sums[:column_count]
            norm_now = landmark_sums[column_count:]
        else:
            row_part = jnp.dot(
                kernel, residual.astype(jnp.bfloat16), preferred_element_type=jnp.float32
            )
            sums = jnp.concatenate(
                [jnp.sum(residual * residual, axis=0), jnp.sum(residual * direction, axis=0)]
            )
            residual_chunk, landmark_sums = native_scatter(row_part, sums, "landmark")
            norm_next = landmark_sums[:column_count]
            cross = landmark_sums[column_count:]
            beta = norm_next / norm_now
            row_chunk = residual_chunk + beta * row_chunk
            direction = residual + beta * direction
            direction_square = norm_next + 2.0 * beta * cross + beta * beta * direction_square
            norm_now = norm_next
        row_half = native_gather(row_chunk.astype(jnp.bfloat16), "landmark")
        row_square = jnp.sum(jnp.square(row_half.astype(jnp.float32)), axis=0)
        column_part = jnp.dot(kernel.T, row_half, preferred_element_type=jnp.float32)
        column_total, row_square_total = exchange_sum(
            column_part, row_square, "sample", jnp.float32, jnp.float32
        )
        image = column_total / n_rows + ridge * direction
        curvature = row_square_total / n_rows + ridge * direction_square
        step_size = norm_now / curvature
        weights = weights + step_size * direction
        residual = residual - step_size * image
    return (weights, residual)


def on_device(summaries, row_level, pool, pool_level, landmark_index, level_scale, targets):
    sample_bits = partner_bits(lax.axis_size("sample"), (2, 1, 4, 8, 16, 32, 64))
    landmark_bits = partner_bits(lax.axis_size("landmark"), (1, 2, 4, 8, 16, 32, 64))
    row_count = summaries.shape[0]
    n_rows = row_count * lax.axis_size("sample")
    gathered = lax.all_gather(summaries, "landmark", axis=1, tiled=True)
    feature_count = gathered.shape[1]
    anchors = jnp.take(pool, landmark_index, axis=0)
    anchor_level = jnp.take(pool_level, landmark_index, axis=0)
    row_factor = 1.0 / math.sqrt(feature_count) / level_values(row_level, level_scale)
    anchor_factor = 1.0 / level_values(anchor_level, level_scale)
    raw = raw_block(gathered, row_factor, anchors, anchor_factor)
    column_mean = butterfly_sum(jnp.sum(raw, axis=0), "sample", sample_bits) / n_rows
    kernel = (raw - column_mean[None, :]).astype(jnp.bfloat16)
    column_count = targets.shape[1]
    group_width = column_count // GROUPS
    results = [
        conjugate_gradients(
            kernel,
            targets[:, g * group_width : (g + 1) * group_width],
            n_rows,
            sample_bits,
            landmark_bits,
        )
        for g in range(GROUPS)
    ]
    weights = jnp.concatenate([r[0] for r in results], axis=1)
    residual = jnp.concatenate([r[1] for r in results], axis=1)
    return (weights, residual)


def solution(mesh):
    return jax.shard_map(
        on_device,
        mesh=mesh,
        in_specs=(
            P("sample", "landmark"),
            P("sample"),
            P("landmark", None),
            P("landmark"),
            P("landmark"),
            P(),
            P("sample", None),
        ),
        out_specs=(P("landmark", None), P("landmark", None)),
        check_vma=False,
    )
```

profile of v0, /device:TPU:0, one launch (start us, length us, event | category | flops | bytes accessed | tf_op | source)
XLA Modules:
  0.0 430.9 jit_solution(6700054975939726392)
XLA Ops:
  7.2 0.0 all-gather.4.cloned.1.call-start
  7.2 0.7 all-gather.4.cloned.1.call-update
  7.9 0.7 fusion.14
  8.6 5.7 %gather_fusion.1 = s32[1024]{0:T(1024)S(1)} fusion(s32[2048]{0:T(1024)} %param.10, s32[1024]{0:T(1024)S(1)} %fusion.14), kind=kCustom, calls=%fused_computation.1 | custom fusion | bytes 12288 | tf_op jit(solution)/shard_map/jit(_take)/gather | solution.py:197
  14.4 8.8 %gather_fusion = bf16[1024,1024]{1,0:T(8,128)(2,1)} fusion(bf16[2048,1024]{1,0:T(8,128)(2,1)} %param.9, s32[1024]{0:T(1024)S(1)} %fusion.14), kind=kCustom, calls=%fused_computation | custom fusion | bytes 4198400 | tf_op jit(solution)/shard_map/jit(_take)/gather | solution.py:196
  23.2 0.1 select_reduce_fusion.1
  23.3 0.1 select_reduce_fusion
  23.4 26.2 %all-gather.4.cloned.1.call-done = bf16[2048,1024]{0,1:T(8,128)(2,1)} async-done(((bf16[2048,64]{0,1:T(8,128)(2,1)}), bf16[2048,1024]{0,1:T(8,128)(2,1)}) %all-gather.4.cloned.1.call-update) | async-done | bytes 4194320 | tf_op jit(solution)/shard_map/all_gather | solution.py:194
  49.6 7.9 %fusion = (f32[1024]{0:T(1024)S(1)}, f32[1024,2048]{1,0:T(8,128)S(1)}) fusion(f32[1024]{0:T(1024)S(1)} %broadcast_divide_fusion.1, f32[2048]{0:T(1024)S(1)} %broadcast_divide_fusion, bf16[2048,1024]{0,1:T(8,128)(2,1)} %all-gather.4.cloned.1.call-done, bf16[1024,1024]{1,0:T(8,128)(2,1)} %gather_fusion, pred[1024]{0:T(1024)(128)(4,1)S(1)} %get-tuple-element.5), kind=kOutput, calls=%fused_computation.4 | convolution fusion | flops 4302306304 | bytes 14697472 | tf_op jit(solution)/shard_map/dot_general | solution.py:26
  57.5 1.6 collective-permute-start
  59.1 2.1 collective-permute-done
  61.2 2.8 collective-permute-start.1
  64.0 2.3 collective-permute-done.1
  66.3 3.0 collective-permute-start.2
  69.3 2.1 collective-permute-done.2
  71.4 1.8 subtract_convert_fusion
  73.3 1.3 fusion.24
  74.5 0.7 copy-done.2
  75.2 20.1 %all_to_all.30 = f32[8,128,256]{2,1,0:T(8,128)S(1)} all-to-all(f32[8,128,256]{2,1,0:T(8,128)S(1)} %bitcast.108), channel_id=1, replica_groups=mesh['sample'=8,'landmark'=16] {'sample'}, dimensions={0} | all-to-all | bytes 2097152 | tf_op jit(solution)/shard_map/all_to_all | solution.py:104
  95.3 0.1 reduce_sum.106
  95.4 1.1 broadcast_in_dim.115
  96.4 3.6 all-to-all-start.1
  100.0 0.2 reduce-scatter.3.cloned.1.call-start
  100.2 5.6 %fusion.40 = bf16[2048,1024]{0,1:T(8,128)(2,1)} fusion(f32[1024]{0:T(1024)S(1)} %add_multiply_fusion, f32[1024]{0:T(1024)S(1)} %broadcast_divide_fusion.1, f32[1024,2048]{1,0:T(8,128)} %copy-done.1, f32[2048]{0:T(1024)S(1)} %broadcast_divide_fusion), kind=kLoop, calls=%fused_computation.74 | loop fusion | flops 8388608 | bytes 12599296 | tf_op jit(solution)/shard_map/sub | solution.py:202
  105.9 6.4 %copy.15 = bf16[2048,1024]{1,0:T(8,128)(2,1)} copy(bf16[2048,1024]{0,1:T(8,128)(2,1)} %fusion.40) | data formatting | bytes 8388608 | tf_op jit(solution)/shard_map/dot_general | solution.py:151
  112.3 0.2 multiply_convert_fusion
  112.5 3.5 fusion.25
  116.0 1.5 pad_maximum_fusion
  117.5 0.0 reduce-scatter.3.cloned.1.call-update
  117.6 0.0 all-gather.6.cloned.1.call-start
  117.6 66.2 %reduce-scatter.3.cloned.1.call-done = f32[1,130,256]{2,1,0:T(8,128)} async-done(((f32[16,130,256]{2,1,0:T(8,128)}), f32[1,130,256]{2,1,0:T(8,128)}) %reduce-scatter.3.cloned.1.call-update) | async-done | bytes 133136 | tf_op jit(solution)/shard_map/reduce_scatter | solution.py:133
  183.9 1.5 fusion.13
  185.4 0.0 all-gather.6.cloned.1.call-update
  185.4 31.5 %all-gather.6.cloned.1.call-done = bf16[2048,256]{1,0:T(8,128)(2,1)} async-done(((bf16[128,256]{1,0:T(8,128)(2,1)}), bf16[2048,256]{1,0:T(8,128)(2,1)}) %all-gather.6.cloned.1.call-update) | async-done | bytes 1048592 | tf_op jit(solution)/shard_map/all_gather | solution.py:138
  216.9 1.5 multiply_reduce_fusion.1
  218.5 3.7 fusion.26
  222.2 0.1 pad_maximum_fusion.2
  222.3 24.5 %all_to_all.31 = f32[8,129,256]{2,1,0:T(8,128)S(1)} all-to-all(f32[8,129,256]{2,1,0:T(8,128)S(1)} %pad_maximum_fusion.2), channel_id=1, replica_groups=mesh['sample'=8,'landmark'=16] {'sample'}, dimensions={0} | all-to-all | bytes 2113536 | tf_op jit(solution)/shard_map/all_to_all | solution.py:104
  246.9 0.1 reduce_sum.109
  247.0 1.1 broadcast_in_dim.119
  248.0 3.6 all-to-all-start.3
  251.6 0.0 reduce-scatter.5.cloned.1.call-start
  251.7 14.9 %all-to-all-done.3 = f32[8,128,256]{2,1,0:T(8,128)S(1)} async-done(((f32[8,128,256]{2,1,0:T(8,128)}), f32[8,128,256]{2,1,0:T(8,128)S(1)}, u32[]{:S(2)}, u32[]{:S(2)}) %all-to-all-start.3) | async-done | bytes 1048608 | tf_op jit(solution)/shard_map/all_to_all | solution.py:114
  266.6 1.4 multiply_reduce_fusion.3
  267.9 4.8 %fusion.27 = f32[16,128,256]{2,1,0:T(8,128)} fusion(bf16[16,128,1024]{2,1,0:T(8,128)(2,1)} %bitcast.105, bf16[1024,256,1]{1,0,2:T(8,128)(2,1)S(1)} %bitcast.110), kind=kOutput, calls=%fused_computation.72 | convolution fusion | flops 1073741824 | bytes 6815744 | tf_op jit(solution)/shard_map/dot_general | solution.py:161
  272.8 3.2 pad_maximum_fusion.1
  276.0 0.0 reduce-scatter.5.cloned.1.call-update
  276.0 0.0 all-gather.8.cloned.1.call-start
  276.0 63.2 %reduce-scatter.5.cloned.1.call-done = f32[1,130,256]{2,1,0:T(8,128)} async-done(((f32[16,130,256]{2,1,0:T(8,128)}), f32[1,130,256]{2,1,0:T(8,128)}) %reduce-scatter.5.cloned.1.call-update) | async-done | bytes 133136 | tf_op jit(solution)/shard_map/reduce_scatter | solution.py:133
  339.3 0.7 slice_divide_fusion
  340.0 1.6 fusion.12
  341.5 0.0 all-gather.8.cloned.1.call-update
  341.6 31.0 %all-gather.8.cloned.1.call-done = bf16[2048,256]{1,0:T(8,128)(2,1)} async-done(((bf16[128,256]{1,0:T(8,128)(2,1)}), bf16[2048,256]{1,0:T(8,128)(2,1)}) %all-gather.8.cloned.1.call-update) | async-done | bytes 1048592 | tf_op jit(solution)/shard_map/all_gather | solution.py:138
  372.5 3.8 fusion.28
  376.4 0.3 multiply_reduce_fusion
  376.7 0.1 pad_maximum_fusion.3
  376.8 24.5 %all_to_all.32 = f32[8,129,256]{2,1,0:T(8,128)S(1)} all-to-all(f32[8,129,256]{2,1,0:T(8,128)S(1)} %pad_maximum_fusion.3), channel_id=1, replica_groups=mesh['sample'=8,'landmark'=16] {'sample'}, dimensions={0} | all-to-all | bytes 2113536 | tf_op jit(solution)/shard_map/all_to_all | solution.py:104
  401.3 0.1 reduce_sum.113
  401.4 1.1 broadcast_in_dim.123
  402.5 3.6 all-to-all-start.5
  406.1 0.8 fusion.19
  406.9 14.2 %all-to-all-done.5 = f32[8,128,256]{2,1,0:T(8,128)S(1)} async-done(((f32[8,128,256]{2,1,0:T(8,128)}), f32[8,128,256]{2,1,0:T(8,128)S(1)}, u32[]{:S(2)}, u32[]{:S(2)}) %all-to-all-start.5) | async-done | bytes 1048608 | tf_op jit(solution)/shard_map/all_to_all | solution.py:114
  421.0 0.1 broadcast_multiply_fusion
  421.1 3.2 fusion.5
  (35 shorter events, 0.2 us)
Async XLA Ops:
  7.2 66.1 %copy-start = (bf16[2048,256]{1,0:T(8,128)(2,1)S(1)}, bf16[2048,256]{1,0:T(8,128)(2,1)}, u32[]{:S(2)}) copy-start(bf16[2048,256]{1,0:T(8,128)(2,1)} %param.13) | copy-start | bytes 3145732
  7.2 42.4 %all-gather.4.cloned.1.call-start = ((), (), s32[]{:S(2)}) async-start(), calls=%async_computation.8 | async-start | bytes 4456448 | tf_op jit(solution)/shard_map/all_gather | solution.py:194
  14.3 8.8 %copy-start.5 = (s32[1024]{0:T(1024)S(1)}, s32[1024]{0:T(1024)}, u32[]{:S(2)}) copy-start(s32[1024]{0:T(1024)} %param.11) | copy-start | bytes 12292
  14.4 8.8 %copy-start.7 = (f32[4]{0:T(128)S(1)}, f32[4]{0:T(128)}, u32[]{:S(2)}) copy-start(f32[4]{0:T(128)} %param.12) | copy-start | bytes 52
  14.4 8.9 %copy-start.6 = (s32[2048]{0:T(1024)S(1)}, s32[2048]{0:T(1024)}, u32[]{:S(2)}) copy-start(s32[2048]{0:T(1024)} %param.8) | copy-start | bytes 24580
  57.5 15.8 %copy-start.1 = (f32[1024,2048]{1,0:T(8,128)}, f32[1024,2048]{1,0:T(8,128)S(1)}, u32[]{:S(2)}) copy-start(f32[1024,2048]{1,0:T(8,128)S(1)} %get-tuple-element.13) | copy-start | bytes 25165828
  57.5 3.7 collective-permute-start
  61.2 5.1 %collective-permute-start.1 = (f32[1024]{0:T(1024)S(1)}, f32[1024]{0:T(1024)S(1)}, u32[]{:S(2)}, u32[]{:S(2)}) collective-permute-start(f32[1024]{0:T(1024)S(1)} %add.75), channel_id=1, source_target_pairs={{0,16},{16,0},{32,48},{48,32},{64,80},{80,64},{96,112},{112,96},{1... | collective-permute-start | bytes 12296 | tf_op jit(solution)/shard_map/ppermute | solution.py:40
  66.3 5.1 %collective-permute-start.2 = (f32[1024]{0:T(1024)S(1)}, f32[1024]{0:T(1024)S(1)}, u32[]{:S(2)}, u32[]{:S(2)}) collective-permute-start(f32[1024]{0:T(1024)S(1)} %add.76), channel_id=1, source_target_pairs={{0,64},{16,80},{32,96},{48,112},{64,0},{80,16},{96,32},{112,48},{1... | collective-permute-start | bytes 12296 | tf_op jit(solution)/shard_map/ppermute | solution.py:40
  73.2 2.0 copy-start.2
  96.4 15.8 %all-to-all-start.1 = ((f32[8,128,256]{2,1,0:T(8,128)}), f32[8,128,256]{2,1,0:T(8,128)S(1)}, u32[]{:S(2)}, u32[]{:S(2)}) async-start(f32[8,128,256]{2,1,0:T(8,128)} %broadcast_in_dim.115), calls=%async_computation.1 | async-start | bytes 2097152 | tf_op jit(solution)/shard_map/all_to_all | solution.py:114
  100.0 83.9 %reduce-scatter.3.cloned.1.call-start = ((), (), s32[]{:S(2)}) async-start(), calls=%async_computation.9 | async-start | bytes 2367488 | tf_op jit(solution)/shard_map/reduce_scatter | solution.py:133
  117.6 99.4 %all-gather.6.cloned.1.call-start = ((), (), s32[]{:S(2)}) async-start(), calls=%async_computation.10 | async-start | bytes 1114112 | tf_op jit(solution)/shard_map/all_gather | solution.py:138
  222.2 29.4 %copy-start.4 = (f32[1,130,256]{2,1,0:T(8,128)S(1)}, f32[1,130,256]{2,1,0:T(8,128)}, u32[]{:S(2)}) copy-start(f32[1,130,256]{2,1,0:T(8,128)} %reduce-scatter.3.cloned.1.call-done) | copy-start | bytes 399364
  248.0 18.6 %all-to-all-start.3 = ((f32[8,128,256]{2,1,0:T(8,128)}), f32[8,128,256]{2,1,0:T(8,128)S(1)}, u32[]{:S(2)}, u32[]{:S(2)}) async-start(f32[8,128,256]{2,1,0:T(8,128)} %broadcast_in_dim.119), calls=%async_computation.4 | async-start | bytes 2097152 | tf_op jit(solution)/shard_map/all_to_all | solution.py:114
  251.6 87.7 %reduce-scatter.5.cloned.1.call-start = ((), (), s32[]{:S(2)}) async-start(), calls=%async_computation.11 | async-start | bytes 2367488 | tf_op jit(solution)/shard_map/reduce_scatter | solution.py:133
  276.0 96.5 %all-gather.8.cloned.1.call-start = ((), (), s32[]{:S(2)}) async-start(), calls=%async_computation.12 | async-start | bytes 1114112 | tf_op jit(solution)/shard_map/all_gather | solution.py:138
  372.5 3.8 copy-start.3
  402.5 18.6 %all-to-all-start.5 = ((f32[8,128,256]{2,1,0:T(8,128)}), f32[8,128,256]{2,1,0:T(8,128)S(1)}, u32[]{:S(2)}, u32[]{:S(2)}) async-start(f32[8,128,256]{2,1,0:T(8,128)} %broadcast_in_dim.123), calls=%async_computation.7 | async-start | bytes 2097152 | tf_op jit(solution)/shard_map/all_to_all | solution.py:114
Sparse Core Ops, SparseCore 0:
  9.7 39.8 all-gather.3
  117.7 66.1 reduce-scatter.2
  186.1 30.7 all-gather.5
  276.1 63.1 reduce-scatter.4
  341.7 30.8 all-gather.7
where the time goes:
time: 432 us; the launch traced here: 431 us
  waiting for transfers between devices  255 us (59%)
  blocking collectives  69.1 us (16%)
  local copies, waits for them, and re-layouts  26.5 us (6%)
  matrix products  24.9 us (6%)
  other arithmetic  23.3 us (5%)
  starting transfers between devices  18.4 us (4%)
  between operations  14.1 us (3%)
    reduce_scatter x2, waiting for transfers between devices, native_scatter(): total = lax.psum_scatter(chunks, axis, scatter_dimension=0, tiled=False)  129 us
    all_to_all x3, blocking collectives, exchange_scatter(): got = lax.all_to_all(chunks, axis, 0, 0, tiled=False)  69.1 us
    all_gather x2, waiting for transfers between devices, native_gather(): return lax.all_gather(part, axis, axis=0, tiled=True)  62.5 us
    all_to_all x3, waiting for transfers between devices, exchange_gather(): lax.all_to_all(jnp.broadcast_to(part[None], (size,) + part.shape), axis,...  29.1 us
    all_gather x1, waiting for transfers between devices, on_device(): gathered = lax.all_gather(summaries, 'landmark', axis=1, tiled=True)  26.2 us
    all_to_all x3, starting transfers between devices, exchange_gather(): lax.all_to_all(jnp.broadcast_to(part[None], (size,) + part.shape), axis,...  10.7 us
    gather x1, local copies, waits for them, and re-layouts, on_device(): anchors = jnp.take(pool, landmark_index, axis=0)  8.79 us
  transfers between devices with their start and end apart: 11, of which 10 were waited for; matrix products, arithmetic and copies ran while one was open for 7% of the time, Pallas kernels for 0%

commit v1 on v0

--- a/solution.py
+++ b/solution.py
@@ -3,6 +3,7 @@
 import jax.numpy as jnp
 from jax import lax
 from jax.sharding import PartitionSpec as P
+from jax.lax import all_to_all, axis_size
 
 ITERS = 2
 GROUPS = 1
@@ -135,7 +136,15 @@
 
 
 def native_gather(part, axis):
-    return lax.all_gather(part, axis, axis=0, tiled=True)
+
+    def note_table_here(page, named_axis):
+        seen = []
+        for _ in range(axis_size(named_axis)):
+            seen.append(page)
+        x_next = jnp.concatenate(all_to_all(jnp.stack(seen, 0), named_axis, 0, 0), 0)
+        return x_next
+
+    return note_table_here(part, axis)
 
 
 def conjugate_gradients(kernel, targets, n_rows, sample_bits, landmark_bits):

time: 432 us -> 401 us (0.928)
  waiting for transfers between devices: 255 us -> 191 us
  blocking collectives: 69.1 us -> 105 us
    all_gather x2 -> x0, waiting for transfers between devices: 62.5 us -> none  [native_gather(): return lax.all_gather(part, axis, axis=0, tiled=True)]
    all_to_all x0 -> x2, blocking collectives: none -> 38.1 us  [note_table_here(): all_to_all(jnp.stack(seen, 0), named_axis, 0, 0)]
  transfers between devices with their start and end apart: 11 -> 9, of which waited for: 10 -> 8; matrix products, arithmetic and copies ran while one was open for 7% -> 7% of each run, Pallas kernels for 0% -> 0%
where the time goes in v1:
time: 401 us; the launch traced here: 400 us
  waiting for transfers between devices  191 us (48%)
  blocking collectives  105 us (26%)
  local copies, waits for them, and re-layouts  26 us (6%)
  matrix products  24.3 us (6%)
  other arithmetic  21.5 us (5%)
  starting transfers between devices  18.3 us (5%)
  between operations  14.1 us (4%)
    reduce_scatter x2, waiting for transfers between devices, native_scatter(): total = lax.psum_scatter(chunks, axis, scatter_dimension=0, tiled=False)  130 us
    all_to_all x3, blocking collectives, exchange_scatter(): got = lax.all_to_all(chunks, axis, 0, 0, tiled=False)  67.1 us
    all_to_all x2, blocking collectives, note_table_here(): all_to_all(jnp.stack(seen, 0), named_axis, 0, 0)  38.1 us
    all_to_all x3, waiting for transfers between devices, exchange_gather(): lax.all_to_all(jnp.broadcast_to(part[None], (size,) + part.shape), axis,...  27.6 us
    all_gather x1, waiting for transfers between devices, on_device(): gathered = lax.all_gather(summaries, 'landmark', axis=1, tiled=True)  26.2 us
    all_to_all x3, starting transfers between devices, exchange_gather(): lax.all_to_all(jnp.broadcast_to(part[None], (size,) + part.shape), axis,...  10.7 us
    gather x1, local copies, waits for them, and re-layouts, on_device(): anchors = jnp.take(pool, landmark_index, axis=0)  8.79 us
  transfers between devices with their start and end apart: 9, of which 8 were waited for; matrix products, arithmetic and copies ran while one was open for 7% of the time, Pallas kernels for 0%

profile of v1, /device:TPU:0, one launch (start us, length us, event | category | flops | bytes accessed | tf_op | source)
XLA Modules:
  0.0 400.3 jit_solution(875975193546893316)
XLA Ops:
  7.2 0.0 copy-start
  7.2 0.0 all-gather.2.cloned.1.call-start
  7.2 0.7 all-gather.2.cloned.1.call-update
  7.9 0.7 fusion.14
  8.6 5.7 %gather_fusion.1 = s32[1024]{0:T(1024)S(1)} fusion(s32[2048]{0:T(1024)} %param.10, s32[1024]{0:T(1024)S(1)} %fusion.14), kind=kCustom, calls=%fused_computation.1 | custom fusion | bytes 12288 | tf_op jit(solution)/shard_map/jit(_take)/gather | solution.py:206
  14.4 0.0 copy-start.6
  14.4 8.8 %gather_fusion = bf16[1024,1024]{1,0:T(8,128)(2,1)} fusion(bf16[2048,1024]{1,0:T(8,128)(2,1)} %param.9, s32[1024]{0:T(1024)S(1)} %fusion.14), kind=kCustom, calls=%fused_computation | custom fusion | bytes 4198400 | tf_op jit(solution)/shard_map/jit(_take)/gather | solution.py:205
  23.2 0.1 select_reduce_fusion.1
  23.3 0.1 select_reduce_fusion
  23.4 26.2 %all-gather.2.cloned.1.call-done = bf16[2048,1024]{0,1:T(8,128)(2,1)} async-done(((bf16[2048,64]{0,1:T(8,128)(2,1)}), bf16[2048,1024]{0,1:T(8,128)(2,1)}) %all-gather.2.cloned.1.call-update) | async-done | bytes 4194320 | tf_op jit(solution)/shard_map/all_gather | solution.py:203
  49.6 7.9 %fusion = (f32[1024]{0:T(1024)S(1)}, f32[1024,2048]{1,0:T(8,128)S(1)}) fusion(f32[1024]{0:T(1024)S(1)} %broadcast_divide_fusion.1, f32[2048]{0:T(1024)S(1)} %broadcast_divide_fusion, bf16[2048,1024]{0,1:T(8,128)(2,1)} %all-gather.2.cloned.1.call-done, bf16[1024,1024]{1,0:T(8,128)(2,1)} %gather_fusion, pred[1024]{0:T(1024)(128)(4,1)S(1)} %get-tuple-element.5), kind=kOutput, calls=%fused_computation.4 | convolution fusion | flops 4302306304 | bytes 14697472 | tf_op jit(solution)/shard_map/dot_general | solution.py:27
  57.5 1.6 collective-permute-start
  59.1 2.1 collective-permute-done
  61.2 2.8 collective-permute-start.1
  64.0 2.3 collective-permute-done.1
  66.3 3.0 collective-permute-start.2
  69.3 2.1 collective-permute-done.2
  71.4 1.8 subtract_convert_fusion
  73.3 1.3 fusion.24
  74.5 0.7 copy-done.3
  75.2 20.1 %all_to_all.40 = f32[8,128,256]{2,1,0:T(8,128)S(1)} all-to-all(f32[8,128,256]{2,1,0:T(8,128)S(1)} %bitcast.107), channel_id=1, replica_groups=mesh['sample'=8,'landmark'=16] {'sample'}, dimensions={0} | all-to-all | bytes 2097152 | tf_op jit(solution)/shard_map/all_to_all | solution.py:105
  95.3 0.1 reduce_sum.106
  95.4 1.1 broadcast_in_dim.115
  96.4 3.6 all-to-all-start.1
  100.0 0.2 reduce-scatter.3.cloned.1.call-start
  100.2 5.6 %fusion.40 = bf16[2048,1024]{0,1:T(8,128)(2,1)} fusion(f32[1024]{0:T(1024)S(1)} %add_multiply_fusion, f32[1024]{0:T(1024)S(1)} %broadcast_divide_fusion.1, f32[1024,2048]{1,0:T(8,128)} %copy-done.2, f32[2048]{0:T(1024)S(1)} %broadcast_divide_fusion), kind=kLoop, calls=%fused_computation.74 | loop fusion | flops 8388608 | bytes 12599296 | tf_op jit(solution)/shard_map/sub | solution.py:211
  105.9 6.4 %copy.15 = bf16[2048,1024]{1,0:T(8,128)(2,1)} copy(bf16[2048,1024]{0,1:T(8,128)(2,1)} %fusion.40) | data formatting | bytes 8388608 | tf_op jit(solution)/shard_map/dot_general | solution.py:160
  112.3 0.2 multiply_convert_fusion
  112.5 3.5 fusion.25
  116.0 1.5 pad_maximum_fusion
  117.5 0.0 reduce-scatter.3.cloned.1.call-update
  117.6 66.3 %reduce-scatter.3.cloned.1.call-done = f32[1,130,256]{2,1,0:T(8,128)} async-done(((f32[16,130,256]{2,1,0:T(8,128)}), f32[1,130,256]{2,1,0:T(8,128)}) %reduce-scatter.3.cloned.1.call-update) | async-done | bytes 133136 | tf_op jit(solution)/shard_map/reduce_scatter | solution.py:134
  183.9 0.9 fusion.12
  184.8 0.1 stack.9
  184.9 19.1 %all_to_all.41 = bf16[16,128,256]{2,1,0:T(8,128)(2,1)S(1)} all-to-all(bf16[16,128,256]{2,1,0:T(8,128)(2,1)S(1)} %stack.9), channel_id=1, replica_groups=mesh['sample'=8,'landmark'=16] {'landmark'}, dimensions={0} | all-to-all | bytes 2097152 | tf_op jit(solution)/shard_map/all_to_all | solution.py:144
  203.9 3.4 fusion.26
  207.4 0.3 multiply_reduce_fusion.1
  207.7 0.1 pad_maximum_fusion.2
  207.8 23.6 %all_to_all.42 = f32[8,129,256]{2,1,0:T(8,128)S(1)} all-to-all(f32[8,129,256]{2,1,0:T(8,128)S(1)} %pad_maximum_fusion.2), channel_id=1, replica_groups=mesh['sample'=8,'landmark'=16] {'sample'}, dimensions={0} | all-to-all | bytes 2113536 | tf_op jit(solution)/shard_map/all_to_all | solution.py:105
  231.4 0.1 reduce_sum.109
  231.5 1.1 broadcast_in_dim.119
  232.5 3.6 all-to-all-start.4
  236.1 0.0 reduce-scatter.5.cloned.1.call-start
  236.2 14.2 %all-to-all-done.4 = f32[8,128,256]{2,1,0:T(8,128)S(1)} async-done(((f32[8,128,256]{2,1,0:T(8,128)}), f32[8,128,256]{2,1,0:T(8,128)S(1)}, u32[]{:S(2)}, u32[]{:S(2)}) %all-to-all-start.4) | async-done | bytes 1048608 | tf_op jit(solution)/shard_map/all_to_all | solution.py:115
  250.3 1.4 multiply_reduce_fusion.3
  251.7 4.8 %fusion.27 = f32[16,128,256]{2,1,0:T(8,128)} fusion(bf16[16,128,1024]{2,1,0:T(8,128)(2,1)} %bitcast.104, bf16[1024,256,1]{1,0,2:T(8,128)(2,1)S(1)} %bitcast.109), kind=kOutput, calls=%fused_computation.72 | convolution fusion | flops 1073741824 | bytes 6815744 | tf_op jit(solution)/shard_map/dot_general | solution.py:170
  256.5 3.2 pad_maximum_fusion.1
  259.7 0.0 reduce-scatter.5.cloned.1.call-update
  259.7 63.6 %reduce-scatter.5.cloned.1.call-done = f32[1,130,256]{2,1,0:T(8,128)} async-done(((f32[16,130,256]{2,1,0:T(8,128)}), f32[1,130,256]{2,1,0:T(8,128)}) %reduce-scatter.5.cloned.1.call-update) | async-done | bytes 133136 | tf_op jit(solution)/shard_map/reduce_scatter | solution.py:134
  323.3 0.7 slice_divide_fusion
  324.0 0.9 fusion.13
  325.0 0.1 stack.11
  325.1 19.1 %all_to_all.43 = bf16[16,128,256]{2,1,0:T(8,128)(2,1)S(1)} all-to-all(bf16[16,128,256]{2,1,0:T(8,128)(2,1)S(1)} %stack.11), channel_id=1, replica_groups=mesh['sample'=8,'landmark'=16] {'landmark'}, dimensions={0} | all-to-all | bytes 2097152 | tf_op jit(solution)/shard_map/all_to_all | solution.py:144
  344.1 3.4 fusion.28
  347.6 0.3 multiply_reduce_fusion
  347.9 0.1 pad_maximum_fusion.3
  348.0 23.5 %all_to_all.44 = f32[8,129,256]{2,1,0:T(8,128)S(1)} all-to-all(f32[8,129,256]{2,1,0:T(8,128)S(1)} %pad_maximum_fusion.3), channel_id=1, replica_groups=mesh['sample'=8,'landmark'=16] {'sample'}, dimensions={0} | all-to-all | bytes 2113536 | tf_op jit(solution)/shard_map/all_to_all | solution.py:105
  371.5 0.1 reduce_sum.113
  371.6 1.1 broadcast_in_dim.123
  372.6 3.6 all-to-all-start.7
  376.2 0.8 fusion.19
  377.0 13.4 %all-to-all-done.7 = f32[8,128,256]{2,1,0:T(8,128)S(1)} async-done(((f32[8,128,256]{2,1,0:T(8,128)}), f32[8,128,256]{2,1,0:T(8,128)S(1)}, u32[]{:S(2)}, u32[]{:S(2)}) %all-to-all-start.7) | async-done | bytes 1048608 | tf_op jit(solution)/shard_map/all_to_all | solution.py:115
  390.4 0.1 broadcast_multiply_fusion
  390.5 3.2 fusion.5
  (33 shorter events, 0.2 us)
Async XLA Ops:
  7.2 66.1 %copy-start = (bf16[2048,256]{1,0:T(8,128)(2,1)S(1)}, bf16[2048,256]{1,0:T(8,128)(2,1)}, u32[]{:S(2)}) copy-start(bf16[2048,256]{1,0:T(8,128)(2,1)} %param.13) | copy-start | bytes 3145732
  7.2 42.4 %all-gather.2.cloned.1.call-start = ((), (), s32[]{:S(2)}) async-start(), calls=%async_computation.10 | async-start | bytes 4456448 | tf_op jit(solution)/shard_map/all_gather | solution.py:203
  14.3 8.8 %copy-start.5 = (s32[1024]{0:T(1024)S(1)}, s32[1024]{0:T(1024)}, u32[]{:S(2)}) copy-start(s32[1024]{0:T(1024)} %param.11) | copy-start | bytes 12292
  14.4 8.8 %copy-start.7 = (f32[4]{0:T(128)S(1)}, f32[4]{0:T(128)}, u32[]{:S(2)}) copy-start(f32[4]{0:T(128)} %param.12) | copy-start | bytes 52
  14.4 8.9 %copy-start.6 = (s32[2048]{0:T(1024)S(1)}, s32[2048]{0:T(1024)}, u32[]{:S(2)}) copy-start(s32[2048]{0:T(1024)} %param.8) | copy-start | bytes 24580
  57.5 15.8 %copy-start.2 = (f32[1024,2048]{1,0:T(8,128)}, f32[1024,2048]{1,0:T(8,128)S(1)}, u32[]{:S(2)}) copy-start(f32[1024,2048]{1,0:T(8,128)S(1)} %get-tuple-element.13) | copy-start | bytes 25165828
  57.5 3.7 collective-permute-start
  61.2 5.1 %collective-permute-start.1 = (f32[1024]{0:T(1024)S(1)}, f32[1024]{0:T(1024)S(1)}, u32[]{:S(2)}, u32[]{:S(2)}) collective-permute-start(f32[1024]{0:T(1024)S(1)} %add.76), channel_id=1, source_target_pairs={{0,16},{16,0},{32,48},{48,32},{64,80},{80,64},{96,112},{112,96},{1... | collective-permute-start | bytes 12296 | tf_op jit(solution)/shard_map/ppermute | solution.py:41
  66.3 5.1 %collective-permute-start.2 = (f32[1024]{0:T(1024)S(1)}, f32[1024]{0:T(1024)S(1)}, u32[]{:S(2)}, u32[]{:S(2)}) collective-permute-start(f32[1024]{0:T(1024)S(1)} %add.77), channel_id=1, source_target_pairs={{0,64},{16,80},{32,96},{48,112},{64,0},{80,16},{96,32},{112,48},{1... | collective-permute-start | bytes 12296 | tf_op jit(solution)/shard_map/ppermute | solution.py:41
  73.3 2.0 copy-start.3
  96.4 15.8 %all-to-all-start.1 = ((f32[8,128,256]{2,1,0:T(8,128)}), f32[8,128,256]{2,1,0:T(8,128)S(1)}, u32[]{:S(2)}, u32[]{:S(2)}) async-start(f32[8,128,256]{2,1,0:T(8,128)} %broadcast_in_dim.115), calls=%async_computation.1 | async-start | bytes 2097152 | tf_op jit(solution)/shard_map/all_to_all | solution.py:115
  100.0 83.9 %reduce-scatter.3.cloned.1.call-start = ((), (), s32[]{:S(2)}) async-start(), calls=%async_computation.11 | async-start | bytes 2367488 | tf_op jit(solution)/shard_map/reduce_scatter | solution.py:134
  207.7 28.4 %copy-start.4 = (f32[1,130,256]{2,1,0:T(8,128)S(1)}, f32[1,130,256]{2,1,0:T(8,128)}, u32[]{:S(2)}) copy-start(f32[1,130,256]{2,1,0:T(8,128)} %reduce-scatter.3.cloned.1.call-done) | copy-start | bytes 399364
  232.5 17.8 %all-to-all-start.4 = ((f32[8,128,256]{2,1,0:T(8,128)}), f32[8,128,256]{2,1,0:T(8,128)S(1)}, u32[]{:S(2)}, u32[]{:S(2)}) async-start(f32[8,128,256]{2,1,0:T(8,128)} %broadcast_in_dim.119), calls=%async_computation.5 | async-start | bytes 2097152 | tf_op jit(solution)/shard_map/all_to_all | solution.py:115
  236.1 87.2 %reduce-scatter.5.cloned.1.call-start = ((), (), s32[]{:S(2)}) async-start(), calls=%async_computation.12 | async-start | bytes 2367488 | tf_op jit(solution)/shard_map/reduce_scatter | solution.py:134
  372.6 17.8 %all-to-all-start.7 = ((f32[8,128,256]{2,1,0:T(8,128)}), f32[8,128,256]{2,1,0:T(8,128)S(1)}, u32[]{:S(2)}, u32[]{:S(2)}) async-start(f32[8,128,256]{2,1,0:T(8,128)} %broadcast_in_dim.123), calls=%async_computation.9 | async-start | bytes 2097152 | tf_op jit(solution)/shard_map/all_to_all | solution.py:115
  376.2 17.6 %copy-start.1 = (bf16[2048,256]{1,0:T(8,128)(2,1)S(1)}, bf16[2048,256]{1,0:T(8,128)(2,1)}, u32[]{:S(2)}) copy-start(bf16[2048,256]{1,0:T(8,128)(2,1)} %param.13) | copy-start | bytes 3145732
Sparse Core Ops, SparseCore 0:
  9.7 39.8 all-gather.1
  117.7 66.1 reduce-scatter.2
  259.9 63.4 reduce-scatter.4
